TPU v7x, 32 devices: a whole 2x2x4 slice. The times are simulated.
32 devices in a mesh: ctx: 16 (over z, y, x), head: 2 (over core).
Axes of the slice: x: 2, y: 2, z: 4, core: 2. Of those that a mesh axis runs over, the one named last changes fastest.
Arguments:
- queries: bfloat16 [4096, 4096], P('ctx', 'head')
- keys: bfloat16 [4096, 1024], P('ctx', 'head')
- values: bfloat16 [4096, 1024], P('ctx', 'head'), may hold values from -6 to 6
- positions: int32 [4096], P('ctx'), may hold values from 0 to 6143, as said below
- retrieval: int32 [4], replicated, may hold values from 0 to 7, as said below
- yarn_scale: int32 [1], replicated, may hold values from 2 to 8
- out_weight: bfloat16 [4096, 4096], P('head', 'ctx'), may hold values from -0.125 to 0.125
Outputs:
- layer_out: bfloat16 [4096, 4096], P('ctx', 'head')
Inputs may be any that keep to these rules, and one draw needn't show every extreme that they name: positions start at 0 and rise by 1 or 2 from one token to the next, by 2 at exactly 2048 of the steps. `retrieval`: 4 different KV-head indices.
All inputs are finite; a program needn't handle non-finite values.
Results may differ from a plain program's by a relative error of at most 0.014.
The roundings to bfloat16 on the way count: a program that leaves them out, or rounds other values in their place, can miss the bound.
Values may be sent and summed in bfloat16 or wider, within the bound.
No kernel may reach another device: no remote copies, remote signals or barrier semaphores. Data moves between devices by JAX's collectives and lax.ppermute only.
A program may use at most 128 MiB of HBM per device.

v0:
```python
from functools import partial
import math
import jax
import jax.numpy as jnp
from jax import lax
from jax.sharding import Mesh, PartitionSpec as P

HEAD_SIZE = 128
SINK = 64
WINDOW = 256
ORIG_CTX = 8192
QUERY_PER_KEY = 4
rope_base = 500000.0
neg_big = -1e30


def yarn_tables(positions, yarn_scale):
    half_size = HEAD_SIZE // 2
    factor = yarn_scale[0].astype(jnp.float32)
    freq_index = jnp.arange(half_size, dtype=jnp.float32)
    base_freq = jnp.power(jnp.float32(rope_base), -2.0 * freq_index / HEAD_SIZE)
    wave_ratio = ORIG_CTX * base_freq / (2.0 * math.pi)
    ramp_weight = jnp.clip((wave_ratio - 1.0) / 31.0, 0.0, 1.0)
    yarn_freq = base_freq * ramp_weight + base_freq / factor * (1.0 - ramp_weight)
    angles = positions.astype(jnp.float32)[:, None] * yarn_freq[None, :]
    mscale = 0.1 * jnp.log(factor) + 1.0
    return (jnp.cos(angles) * mscale, jnp.sin(angles) * mscale)


def apply_rotary(x, cosine_lookup, sine_lookup, head_count):
    row_count = x.shape[0]
    shaped = x.astype(jnp.float32).reshape(row_count, head_count, HEAD_SIZE)
    lower_half = shaped[..., : HEAD_SIZE // 2]
    upper_half = shaped[..., HEAD_SIZE // 2 :]
    cosine = cosine_lookup[:, None, :]
    sine_part = sine_lookup[:, None, :]
    rotated = jnp.concatenate(
        [
            lower_half * cosine - upper_half * sine_part,
            upper_half * cosine + lower_half * sine_part,
        ],
        axis=-1,
    )
    return rotated.reshape(row_count, head_count * HEAD_SIZE).astype(jnp.bfloat16)


def update(query_rows, key_block, value_block, visible, partial_state):
    row_max, totals, accum = partial_state
    scores = jnp.einsum(
        "rhgd,khd->hgrk", query_rows, key_block, preferred_element_type=jnp.float32
    ) * (1.0 / math.sqrt(HEAD_SIZE))
    mask_full = visible[:, None]
    scores = jnp.where(mask_full, scores, neg_big)
    new_max = jnp.maximum(row_max, jnp.max(scores, axis=-1))
    weights = jnp.where(mask_full, jnp.exp(scores - new_max[..., None]), 0.0)
    rescale = jnp.exp(row_max - new_max)
    totals = totals * rescale + jnp.sum(weights, axis=-1)
    accum = accum * rescale[..., None] + jnp.einsum(
        "hgrk,khd->hgrd",
        weights.astype(jnp.bfloat16),
        value_block,
        preferred_element_type=jnp.float32,
    )
    return (new_max, totals, accum)


def attend(query_sets, rotated_key, values, flags, kv_local):
    shaped_sets = []
    initial = []
    for query_rows, query_index in query_sets:
        row_count = query_rows.shape[0]
        shaped_sets.append(
            (query_rows.reshape(row_count, kv_local, QUERY_PER_KEY, HEAD_SIZE), query_index)
        )
        initial.append(
            (
                jnp.full((kv_local, QUERY_PER_KEY, row_count), neg_big, jnp.float32),
                jnp.zeros((kv_local, QUERY_PER_KEY, row_count), jnp.float32),
                jnp.zeros((kv_local, QUERY_PER_KEY, row_count, HEAD_SIZE), jnp.float32),
            )
        )
    initial = tuple(initial)
    kv_width = rotated_key.shape[1]
    kv_shard = lax.all_gather(
        jnp.concatenate([rotated_key, values], axis=1), CTX, axis=0, tiled=True
    )
    key_shard = kv_shard[:, :kv_width]
    value_shard = kv_shard[:, kv_width:]
    shard_rows = key_shard.shape[0]
    sub_rows = math.gcd(shard_rows, 512)
    turn_count = shard_rows // sub_rows

    def one_turn(j, inner_states):
        key_block = lax.dynamic_slice_in_dim(key_shard, j * sub_rows, sub_rows, 0).reshape(
            sub_rows, kv_local, HEAD_SIZE
        )
        value_block = lax.dynamic_slice_in_dim(value_shard, j * sub_rows, sub_rows, 0).reshape(
            sub_rows, kv_local, HEAD_SIZE
        )
        key_index = j * sub_rows + jnp.arange(sub_rows, dtype=jnp.int32)
        updated = []
        for (query_rows, query_index), partial_state in zip(shaped_sets, inner_states):
            causal = key_index[None, :] <= query_index[:, None]
            nearby = (key_index[None, :] < SINK) | (
                key_index[None, :] > query_index[:, None] - WINDOW
            )
            visible = causal[None] & (flags[:, None, None] | nearby[None])
            updated.append(
                lax.cond(
                    jnp.any(visible),
                    partial(update, query_rows, key_block, value_block, visible),
                    lambda keep_state: keep_state,
                    partial_state,
                )
            )
        return tuple(updated)

    final = lax.fori_loop(0, turn_count, one_turn, initial)
    results = []
    for (query_rows, query_index), (row_max, totals, accum) in zip(shaped_sets, final):
        output = accum / totals[..., None]
        results.append(
            output.transpose(2, 0, 1, 3)
            .reshape(query_rows.shape[0], kv_local * QUERY_PER_KEY * HEAD_SIZE)
            .astype(jnp.bfloat16)
        )
    return results


CTX = ("cz", "cb")


def head_exchange(x, head_count):
    if head_count == 2:
        other = lax.ppermute(x, "head", [(0, 1), (1, 0)])
        first = lax.axis_index("head") == 0
        return jnp.stack([jnp.where(first, x, other), jnp.where(first, other, x)])
    return lax.all_gather(x, "head", axis=0, tiled=False)


def duo_attend(rotated_query, rotated_key, values, retrieval, kv_local, head_count, ctx_index):
    rows = rotated_query.shape[0]
    ctx_count = lax.psum(1, CTX)
    kv_total = kv_local * head_count
    ret_count = retrieval.shape[0]
    ret_per = ret_count // head_count
    run_per = (kv_total - ret_count) // head_count
    me = lax.axis_index("head")
    is_ret = jnp.any(jnp.arange(kv_total, dtype=jnp.int32)[:, None] == retrieval[None, :], axis=1)
    order = jnp.argsort(is_ret.astype(jnp.int32), stable=True)
    run_ids = lax.dynamic_slice_in_dim(order, me * run_per, run_per)
    ret_ids = lax.dynamic_slice_in_dim(order, kv_total - ret_count + me * ret_per, ret_per)
    q_all = head_exchange(
        rotated_query.reshape(rows, kv_local, QUERY_PER_KEY, HEAD_SIZE), head_count
    )
    q_all = q_all.transpose(1, 0, 2, 3, 4).reshape(rows, kv_total, QUERY_PER_KEY, HEAD_SIZE)
    kv_own = jnp.stack(
        [rotated_key.reshape(rows, kv_local, HEAD_SIZE), values.reshape(rows, kv_local, HEAD_SIZE)],
        axis=2,
    )
    kv_all = head_exchange(kv_own, head_count)
    kv_all = kv_all.transpose(1, 0, 2, 3, 4).reshape(rows, kv_total, 2, HEAD_SIZE)
    own_index = ctx_index * rows + jnp.arange(rows, dtype=jnp.int32)
    inv_root = 1.0 / math.sqrt(HEAD_SIZE)
    run_kv = jnp.take(kv_all, run_ids, axis=1)
    prev_kv = lax.ppermute(run_kv, CTX, [(i, i + 1) for i in range(ctx_count - 1)])
    sink_kv = lax.psum(jnp.where(ctx_index == 0, run_kv[:SINK], jnp.zeros_like(run_kv[:SINK])), CTX)
    near_kv = jnp.concatenate([sink_kv, prev_kv, run_kv], axis=0)
    sink_index = jnp.arange(SINK, dtype=jnp.int32)
    window_index = (ctx_index - 1) * rows + jnp.arange(2 * rows, dtype=jnp.int32)
    causal_sink = sink_index[None, :] <= own_index[:, None]
    in_window = (
        (window_index[None, :] <= own_index[:, None])
        & (window_index[None, :] > own_index[:, None] - WINDOW)
        & (window_index[None, :] >= SINK)
    )
    near_visible = jnp.concatenate([causal_sink, in_window], axis=1)[None]
    q_run = jnp.take(q_all, run_ids, axis=1)
    start = (
        jnp.full((run_per, QUERY_PER_KEY, rows), neg_big, jnp.float32),
        jnp.zeros((run_per, QUERY_PER_KEY, rows), jnp.float32),
        jnp.zeros((run_per, QUERY_PER_KEY, rows, HEAD_SIZE), jnp.float32),
    )
    _, run_totals, run_accum = update(
        q_run, near_kv[:, :, 0], near_kv[:, :, 1], near_visible, start
    )
    run_out = run_accum / run_totals[..., None]
    ret_kv = jnp.take(kv_all, ret_ids, axis=1)
    ret_shard = lax.all_gather(
        ret_kv.reshape(rows, ret_per * 2 * HEAD_SIZE), CTX, axis=0, tiled=True
    )
    ret_shard = ret_shard.reshape(ctx_count * rows, ret_per, 2, HEAD_SIZE)
    q_ret = jnp.take(q_all, ret_ids, axis=1)
    sub_rows = math.gcd(ctx_count * rows, 512)
    turn_count = (ctx_index * rows + rows + sub_rows - 1) // sub_rows

    def one_turn(j, state):
        block = lax.dynamic_slice_in_dim(ret_shard, j * sub_rows, sub_rows, 0)
        key_index = j * sub_rows + jnp.arange(sub_rows, dtype=jnp.int32)
        visible = (key_index[None, :] <= own_index[:, None])[None]
        return update(q_ret, block[:, :, 0], block[:, :, 1], visible, state)

    start = (
        jnp.full((ret_per, QUERY_PER_KEY, rows), neg_big, jnp.float32),
        jnp.zeros((ret_per, QUERY_PER_KEY, rows), jnp.float32),
        jnp.zeros((ret_per, QUERY_PER_KEY, rows, HEAD_SIZE), jnp.float32),
    )
    _, ret_totals, ret_accum = lax.fori_loop(0, turn_count, one_turn, start)
    ret_out = ret_accum / ret_totals[..., None]
    done = jnp.concatenate([ret_out, run_out], axis=0).astype(jnp.bfloat16)
    slots = head_exchange(done, head_count).reshape(kv_total, QUERY_PER_KEY, rows, HEAD_SIZE)
    placed = jnp.concatenate(
        [
            jnp.concatenate(
                [
                    order[
                        kv_total
                        - ret_count
                        + h * ret_per : kv_total
                        - ret_count
                        + (h + 1) * ret_per
                    ],
                    order[h * run_per : (h + 1) * run_per],
                ]
            )
            for h in range(head_count)
        ]
    )
    slot_of = jnp.argsort(placed)
    home = jnp.take(slots, lax.dynamic_slice_in_dim(slot_of, me * kv_local, kv_local), axis=0)
    return home.transpose(2, 0, 1, 3).reshape(rows, kv_local * QUERY_PER_KEY * HEAD_SIZE)


def project(attended, w_local, head_count):
    rows = attended.shape[0]
    col_width = w_local.shape[1]
    plane = lax.psum(1, "cb")
    line = lax.psum(1, "cz")
    a_plane = lax.all_gather(attended, "cb", axis=0, tiled=True)
    w_line = lax.all_gather(w_local, "cz", axis=1, tiled=True)
    part = jnp.dot(a_plane, w_line, preferred_element_type=jnp.float32)
    reduced = lax.psum_scatter(part, "head", scatter_dimension=1, tiled=True).astype(jnp.bfloat16)
    per_head = line // head_count
    pieces = reduced.reshape(plane, rows, per_head * col_width)
    got = lax.all_to_all(pieces, "cb", 0, 0, tiled=False)
    return (
        got.reshape(plane, rows, per_head, col_width)
        .transpose(1, 2, 0, 3)
        .reshape(rows, per_head * plane * col_width)
    )


def shards(queries, keys, values, positions, retrieval, yarn_scale, out_weight):
    rows_dev = queries.shape[0]
    kv_local = keys.shape[1] // HEAD_SIZE
    cosine_lookup, sine_lookup = yarn_tables(positions, yarn_scale)
    rotated_query = apply_rotary(queries, cosine_lookup, sine_lookup, kv_local * QUERY_PER_KEY)
    rotated_key = apply_rotary(keys, cosine_lookup, sine_lookup, kv_local)
    ctx_index = lax.axis_index("cz") * lax.psum(1, "cb") + lax.axis_index("cb")
    head_ids = lax.axis_index("head") * kv_local + jnp.arange(kv_local, dtype=jnp.int32)
    flags = jnp.any(head_ids[:, None] == retrieval[None, :], axis=1)
    own_index = ctx_index * rows_dev + jnp.arange(rows_dev, dtype=jnp.int32)
    head_count = lax.psum(1, "head")
    kv_total = kv_local * head_count
    ret_count = retrieval.shape[0]
    if (
        ret_count % head_count == 0
        and (kv_total - ret_count) % head_count == 0
        and (ret_count < kv_total)
        and (rows_dev >= max(SINK, WINDOW))
    ):
        attended = duo_attend(
            rotated_query, rotated_key, values, retrieval, kv_local, head_count, ctx_index
        )
    else:
        attended = attend(((rotated_query, own_index),), rotated_key, values, flags, kv_local)[0]
    return project(attended, out_weight, head_count)


def grid_of(ctx_count, head_count):
    best = None
    for plane in range(1, ctx_count + 1):
        line = ctx_count // plane
        if ctx_count % plane == 0 and line % head_count == 0 and (plane <= line):
            best = (line, plane)
    return best


def solution(mesh):
    ctx_count = mesh.shape["ctx"]
    head_count = mesh.shape["head"]
    line, plane = grid_of(ctx_count, head_count)
    grid = Mesh(mesh.devices.reshape(line, plane, head_count), ("cz", "cb", "head"))
    return jax.shard_map(
        shards,
        mesh=grid,
        in_specs=(P(CTX, "head"), P(CTX, "head"), P(CTX, "head"), P(CTX), P(), P(), P("head", CTX)),
        out_specs=P(CTX, "head"),
        check_vma=False,
    )
```

profile of v0, /device:TPU:0, one launch (start us, length us, event | category | flops | bytes accessed | tf_op | source)
XLA Modules:
  0.0 394.5 jit_solution(9107826275673010215)
XLA Ops:
  7.2 0.7 convert_element_type.38
  7.9 1.1 copy.33
  9.0 1.1 copy.32
  11.2 0.7 fusion.38
  11.9 1.0 sort.34
  16.1 0.9 copy.35
  18.6 1.4 subtract_convert_fusion
  21.0 5.5 %collective-permute-start.2 = (bf16[256,2,2,128]{3,0,1,2:T(8,128)(2,1)S(1)}, bf16[256,2,2,128]{3,0,1,2:T(8,128)(2,1)}, u32[]{:S(2)}, u32[]{:S(2)}) collective-permute-start(bf16[256,2,2,128]{3,0,1,2:T(8,128)(2,1)S(1)} %fusion.32), channel_id=1, source_target_pairs={{0,2},{2,4},{4,6},{6,8},{8,10},{10,12},{12,14},{14,16},{16,18},{18... | collective-permute-start | bytes 786440 | tf_op jit(solution)/shard_map/ppermute | solution.py:166
  26.6 94.8 %all-reduce.2.cloned.1.call-done = bf16[64,2,2,128]{3,0,1,2:T(8,128)(2,1)} async-done(((bf16[64,2,2,128]{3,0,1,2:T(8,128)(2,1)}), bf16[64,2,2,128]{3,0,1,2:T(8,128)(2,1)}) %all-reduce.2.cloned.1.call-update) | async-done | bytes 65552 | tf_op jit(solution)/shard_map/psum | solution.py:167
  121.4 1.0 pad_maximum_fusion.4
  122.8 1.4 gather_fusion.4
  124.8 2.0 fusion.17
  126.8 1.2 fusion.18
  128.1 2.0 divide_convert_fusion
  130.2 79.8 %all-gather.4.cloned.1.call-done = bf16[4096,512]{0,1:T(8,128)(2,1)} async-done(((bf16[256,512]{0,1:T(8,128)(2,1)}), bf16[4096,512]{0,1:T(8,128)(2,1)}) %all-gather.4.cloned.1.call-update) | async-done | bytes 4194320 | tf_op jit(solution)/shard_map/all_gather | solution.py:189
  210.0 9.7 %while.15 = (s32[]{:T(128)}, f32[2,4,256]{2,1,0:T(4,128)S(1)}, f32[2,4,256]{2,1,0:T(4,128)S(1)}, f32[2,4,256,128]{3,2,1,0:T(8,128)S(1)}, s32[]{:T(128)}, /*index...) while((s32[]{:T(128)}, f32[2,4,256]{2,1,0:T(4,128)S(1)}, ...), condition=%wide.region_6.9_spmd.clone, body=%wide.region_3.8_spmd.clone.sunk | while | flops 551162624 | bytes 33167600 | solution.py:208
  210.4 1.8 fusion.58
  212.3 1.9 copy-done
  214.3 1.0 fusion.59
  215.3 4.4 %fusion.60 = f32[2,4,256,128]{3,2,1,0:T(8,128)S(1)} fusion(f32[2,512,256,4]{2,1,3,0:T(8,128)} %copy-done, f32[2,4,256]{2,1,0:T(4,128)S(1)} %max.13, pred[256,512]{0,1:T(8,128)(4,1)S(1)} %broadcast_compare_fusion.3, f32[2,4,256,128]{3,2,1,0:T(8,128)S(1)} %get-tuple-element.231, f32[2,4,256]{2,1,0:T(4,128)S(1)} %bitcast.163, ...), kind=kOutput, calls=%fused_computation.13.clone.1 | convolution fusion | flops 274202624 | bytes 6701064 | tf_op jit(solution)/shard_map/while/body/hgrk,khd->hgrd/dot_general | solution.py:58
  220.4 1.0 sort.35
  221.4 1.4 collective-permute-done.3
  223.2 0.7 gather_fusion
  224.2 1.3 copy.42
  225.5 64.7 %all-gather.8.cloned.1.call-done = bf16[2048,1024]{1,0:T(8,128)(2,1)} async-done(((bf16[2048,256]{1,0:T(8,128)(2,1)}), bf16[2048,1024]{1,0:T(8,128)(2,1)}) %all-gather.8.cloned.1.call-update) | async-done | bytes 4194320 | tf_op jit(solution)/shard_map/all_gather | solution.py:240
  290.3 52.3 %all-gather.6.cloned.1.call-done = bf16[1024,2048]{0,1:T(8,128)(2,1)} async-done(((bf16[256,2048]{0,1:T(8,128)(2,1)}), bf16[1024,2048]{0,1:T(8,128)(2,1)}) %all-gather.6.cloned.1.call-update) | async-done | bytes 4194320 | tf_op jit(solution)/shard_map/all_gather | solution.py:239
  342.6 10.0 %fusion.47 = f32[1024,1024]{1,0:T(8,128)} fusion(bf16[1024,2048]{0,1:T(8,128)(2,1)} %all-gather.6.cloned.1.call-done, bf16[2048,1024]{1,0:T(8,128)(2,1)} %all-gather.8.cloned.1.call-done), kind=kOutput, calls=%fused_computation.105 | convolution fusion | flops 4294967296 | bytes 12582912 | tf_op jit(solution)/shard_map/dot_general | solution.py:241
  352.7 12.0 %reduce-scatter.2.cloned.1.call-done = f32[1024,512]{1,0:T(8,128)} async-done(((f32[1024,1024]{1,0:T(8,128)}), f32[1024,512]{1,0:T(8,128)}) %reduce-scatter.2.cloned.1.call-update) | async-done | bytes 2097168 | tf_op jit(solution)/shard_map/reduce_scatter | solution.py:242
  364.7 1.7 convert_element_type.43
  366.4 18.3 %all_to_all.5 = bf16[4,256,512]{2,1,0:T(8,128)(2,1)S(1)} all-to-all(bf16[4,256,512]{2,1,0:T(8,128)(2,1)S(1)} %bitcast.148), channel_id=1, replica_groups=mesh['cz'=4,'cb'=4,'head'=2] {'cb'}, dimensions={0} | all-to-all | bytes 2097152 | tf_op jit(solution)/shard_map/all_to_all | solution.py:245
  385.0 1.4 copy.63
  386.3 1.6 reshape.221
  (75 shorter events, 9.7 us)
Async XLA Ops:
  6.5 114.9 %all-reduce.2.cloned.1.call-start = ((), (), s32[]{:S(2)}) async-start(), calls=%async_computation.3 | async-start | bytes 131072 | tf_op jit(solution)/shard_map/psum | solution.py:167
  10.6 2.4 collective-permute-start
  13.2 4.1 %copy-start.1 = (bf16[256,2048]{1,0:T(8,128)(2,1)S(1)}, bf16[256,2048]{1,0:T(8,128)(2,1)}, u32[]{:S(2)}) copy-start(bf16[256,2048]{1,0:T(8,128)(2,1)} %param.13) | copy-start | bytes 3145732
  15.4 194.6 %all-gather.4.cloned.1.call-start = ((), (), s32[]{:S(2)}) async-start(), calls=%async_computation.2 | async-start | bytes 4456448 | tf_op jit(solution)/shard_map/all_gather | solution.py:189
  17.0 273.3 %all-gather.8.cloned.1.call-start = ((), (), s32[]{:S(2)}) async-start(), calls=%async_computation.5 | async-start | bytes 5242880 | tf_op jit(solution)/shard_map/all_gather | solution.py:240
  20.5 101.9 %collective-permute-start.1 = (bf16[256,4,4,128]{3,0,2,1:T(8,128)(2,1)S(1)}, bf16[256,4,4,128]{3,0,2,1:T(8,128)(2,1)S(1)}, u32[]{:S(2)}, u32[]{:S(2)}) collective-permute-start(bf16[256,4,4,128]{3,0,2,1:T(8,128)(2,1)S(1)} %bitcast.146), channel_id=1, source_target_pairs={{0,1},{1,0},{2,3},{3,2},{4,5},{5,4},{6,7},{7,6},{8,9},{9,8},{10,11... | collective-permute-start | bytes 3145736 | tf_op jit(solution)/shard_map/ppermute | solution.py:135
  20.7 321.9 %all-gather.6.cloned.1.call-start = ((), (), s32[]{:S(2)}) async-start(), calls=%async_computation.4 | async-start | bytes 5242880 | tf_op jit(solution)/shard_map/all_gather | solution.py:239
  21.0 100.4 %collective-permute-start.2 = (bf16[256,2,2,128]{3,0,1,2:T(8,128)(2,1)S(1)}, bf16[256,2,2,128]{3,0,1,2:T(8,128)(2,1)}, u32[]{:S(2)}, u32[]{:S(2)}) collective-permute-start(bf16[256,2,2,128]{3,0,1,2:T(8,128)(2,1)S(1)} %fusion.32), channel_id=1, source_target_pairs={{0,2},{2,4},{4,6},{6,8},{8,10},{10,12},{12,14},{14,16},{16,18},{18... | collective-permute-start | bytes 786440 | tf_op jit(solution)/shard_map/ppermute | solution.py:166
  212.3 2.0 copy-start
  220.2 2.7 collective-permute-start.3
  225.5 139.2 %reduce-scatter.2.cloned.1.call-start = ((), (), s32[]{:S(2)}) async-start(), calls=%async_computation.6 | async-start | bytes 6291456 | tf_op jit(solution)/shard_map/reduce_scatter | solution.py:242
Sparse Core Ops, SparseCore 0:
  15.5 105.8 all-reduce.1
  124.1 85.7 all-gather.3
  211.5 78.7 all-gather.7
  292.0 50.6 all-gather.5
  352.8 11.8 reduce-scatter.1
where the time goes:
time: 395 us; the launch traced here: 394 us
  waiting for transfers between devices  305 us (77%)
  matrix products  20.3 us (5%)
  blocking collectives  18.3 us (5%)
  local copies, waits for them, and re-layouts  15.6 us (4%)
  between operations  14.2 us (4%)
  other arithmetic  14.1 us (4%)
  starting transfers between devices  6.47 us (2%)
    psum x1, waiting for transfers between devices, duo_attend(): lax.psum(jnp.where(ctx_index == 0, run_kv[:SINK], jnp.zeros_like(run_kv[:...  94.8 us
    all_gather x1, waiting for transfers between devices, duo_attend(): lax.all_gather(ret_kv.reshape(rows, ret_per * 2 * HEAD_SIZE), CTX, axis=0...  79.8 us
    all_gather x1, waiting for transfers between devices, project(): w_line = lax.all_gather(w_local, 'cz', axis=1, tiled=True)  64.7 us
    all_gather x1, waiting for transfers between devices, project(): a_plane = lax.all_gather(attended, 'cb', axis=0, tiled=True)  52.3 us
    all_to_all x1, blocking collectives, project(): got = lax.all_to_all(pieces, 'cb', 0, 0, tiled=False)  18.3 us
    reduce_scatter x1, waiting for transfers between devices, project(): lax.psum_scatter(part, 'head', scatter_dimension=1, tiled=True)  12 us
    dot_general x1, matrix products, project(): part = jnp.dot(a_plane, w_line, preferred_element_type=jnp.float32)  10 us
  transfers between devices with their start and end apart: 9, of which 6 were waited for; matrix products, arithmetic and copies ran while one was open for 7% of the time, Pallas kernels for 0%

commit v1 on v0

--- a/solution.py
+++ b/solution.py
@@ -164,7 +164,8 @@
     inv_root = 1.0 / math.sqrt(HEAD_SIZE)
     run_kv = jnp.take(kv_all, run_ids, axis=1)
     prev_kv = lax.ppermute(run_kv, CTX, [(i, i + 1) for i in range(ctx_count - 1)])
-    sink_kv = lax.psum(jnp.where(ctx_index == 0, run_kv[:SINK], jnp.zeros_like(run_kv[:SINK])), CTX)
+    u = jnp.where(ctx_index == 0, run_kv[:SINK], jnp.zeros_like(run_kv[:SINK]))
+    sink_kv = jnp.sum(lax.all_gather(u, axis_name=CTX), 0)
     near_kv = jnp.concatenate([sink_kv, prev_kv, run_kv], axis=0)
     sink_index = jnp.arange(SINK, dtype=jnp.int32)
     window_index = (ctx_index - 1) * rows + jnp.arange(2 * rows, dtype=jnp.int32)

time: 395 us -> 349 us (0.88)
  waiting for transfers between devices: 305 us -> 257 us
    psum x1 -> x0, waiting for transfers between devices: 94.8 us -> none  [duo_attend(): lax.psum(jnp.where(ctx_index == 0, run_kv[:SINK], jnp.zeros_like(run_kv[:...]
    all_gather x0 -> x1, waiting for transfers between devices: none -> 45.5 us  [duo_attend(): sink_kv = jnp.sum(lax.all_gather(u, axis_name=CTX), 0)]
  transfers between devices with their start and end apart: 9 -> 9, of which waited for: 6 -> 6; matrix products, arithmetic and copies ran while one was open for 7% -> 8% of each run, Pallas kernels for 0% -> 0%
where the time goes in v1:
time: 349 us; the launch traced here: 348 us
  waiting for transfers between devices  257 us (74%)
  matrix products  19.9 us (6%)
  blocking collectives  18.3 us (5%)
  other arithmetic  16.2 us (5%)
  local copies, waits for them, and re-layouts  15.3 us (4%)
  between operations  14.3 us (4%)
  starting transfers between devices  6.45 us (2%)
    all_gather x1, waiting for transfers between devices, duo_attend(): lax.all_gather(ret_kv.reshape(rows, ret_per * 2 * HEAD_SIZE), CTX, axis=0...  81.1 us
    all_gather x1, waiting for transfers between devices, project(): w_line = lax.all_gather(w_local, 'cz', axis=1, tiled=True)  64.7 us
    all_gather x1, waiting for transfers between devices, project(): a_plane = lax.all_gather(attended, 'cb', axis=0, tiled=True)  52.3 us
    all_gather x1, waiting for transfers between devices, duo_attend(): sink_kv = jnp.sum(lax.all_gather(u, axis_name=CTX), 0)  45.5 us
    all_to_all x1, blocking collectives, project(): got = lax.all_to_all(pieces, 'cb', 0, 0, tiled=False)  18.3 us
    reduce_scatter x1, waiting for transfers between devices, project(): lax.psum_scatter(part, 'head', scatter_dimension=1, tiled=True)  12 us
    dot_general x1, matrix products, project(): part = jnp.dot(a_plane, w_line, preferred_element_type=jnp.float32)  10 us
  transfers between devices with their start and end apart: 9, of which 6 were waited for; matrix products, arithmetic and copies ran while one was open for 8% of the time, Pallas kernels for 0%

profile of v1, /device:TPU:0, one launch (start us, length us, event | category | flops | bytes accessed | tf_op | source)
XLA Modules:
  0.0 348.0 jit_solution(9348527974595854793)
XLA Ops:
  7.9 1.1 copy.33
  9.0 1.1 copy.32
  11.9 1.0 sort.34
  16.4 0.9 copy.35
  18.9 1.4 subtract_convert_fusion
  21.3 5.6 %collective-permute-start.2 = (bf16[256,2,2,128]{3,0,1,2:T(8,128)(2,1)S(1)}, bf16[256,2,2,128]{3,0,1,2:T(8,128)(2,1)}, u32[]{:S(2)}, u32[]{:S(2)}) collective-permute-start(bf16[256,2,2,128]{3,0,1,2:T(8,128)(2,1)S(1)} %fusion.32), channel_id=1, source_target_pairs={{0,2},{2,4},{4,6},{6,8},{8,10},{10,12},{12,14},{14,16},{16,18},{18... | collective-permute-start | bytes 786440 | tf_op jit(solution)/shard_map/ppermute | solution.py:166
  27.2 0.8 gather_fusion.4
  28.0 0.8 gather_fusion.2
  28.7 0.8 select_bitcast_fusion.5
  29.5 45.5 %all-gather.12.cloned.1.call-done = bf16[1024,2,2,128]{3,0,1,2:T(8,128)(2,1)} async-done(((bf16[64,2,2,128]{3,0,1,2:T(8,128)(2,1)}), bf16[1024,2,2,128]{3,0,1,2:T(8,128)(2,1)}) %all-gather.12.cloned.1.call-update) | async-done | bytes 1048592 | tf_op jit(solution)/shard_map/all_gather | solution.py:168
  75.1 1.4 reduce_sum.30
  76.5 1.0 pad_maximum_fusion.4
  77.5 1.6 fusion.17
  79.1 1.2 fusion.18
  80.3 2.0 divide_convert_fusion
  82.3 81.1 %all-gather.6.cloned.1.call-done = bf16[4096,512]{0,1:T(8,128)(2,1)} async-done(((bf16[256,512]{0,1:T(8,128)(2,1)}), bf16[4096,512]{0,1:T(8,128)(2,1)}) %all-gather.6.cloned.1.call-update) | async-done | bytes 4194320 | tf_op jit(solution)/shard_map/all_gather | solution.py:190
  163.5 9.7 %while.15 = (s32[]{:T(128)}, f32[2,4,256]{2,1,0:T(4,128)S(1)}, f32[2,4,256]{2,1,0:T(4,128)S(1)}, f32[2,4,256,128]{3,2,1,0:T(8,128)S(1)}, s32[]{:T(128)}, /*index...) while((s32[]{:T(128)}, f32[2,4,256]{2,1,0:T(4,128)S(1)}, ...), condition=%wide.region_6.9_spmd.clone, body=%wide.region_3.8_spmd.clone.sunk | while | flops 551162624 | bytes 33167600 | solution.py:209
  163.9 1.8 fusion.58
  165.8 1.9 copy-done
  167.7 1.0 fusion.59
  168.8 4.4 %fusion.60 = f32[2,4,256,128]{3,2,1,0:T(8,128)S(1)} fusion(f32[2,512,256,4]{2,1,3,0:T(8,128)} %copy-done, f32[2,4,256]{2,1,0:T(4,128)S(1)} %max.13, pred[256,512]{0,1:T(8,128)(4,1)S(1)} %broadcast_compare_fusion.3, f32[2,4,256,128]{3,2,1,0:T(8,128)S(1)} %get-tuple-element.231, f32[2,4,256]{2,1,0:T(4,128)S(1)} %bitcast.165, ...), kind=kOutput, calls=%fused_computation.13.clone.1 | convolution fusion | flops 274202624 | bytes 6701064 | tf_op jit(solution)/shard_map/while/body/hgrk,khd->hgrd/dot_general | solution.py:58
  173.9 1.0 sort.35
  175.0 1.4 collective-permute-done.3
  177.7 1.3 copy.42
  179.0 64.7 %all-gather.10.cloned.1.call-done = bf16[2048,1024]{1,0:T(8,128)(2,1)} async-done(((bf16[2048,256]{1,0:T(8,128)(2,1)}), bf16[2048,1024]{1,0:T(8,128)(2,1)}) %all-gather.10.cloned.1.call-update) | async-done | bytes 4194320 | tf_op jit(solution)/shard_map/all_gather | solution.py:241
  243.8 52.3 %all-gather.8.cloned.1.call-done = bf16[1024,2048]{0,1:T(8,128)(2,1)} async-done(((bf16[256,2048]{0,1:T(8,128)(2,1)}), bf16[1024,2048]{0,1:T(8,128)(2,1)}) %all-gather.8.cloned.1.call-update) | async-done | bytes 4194320 | tf_op jit(solution)/shard_map/all_gather | solution.py:240
  296.1 10.0 %fusion.47 = f32[1024,1024]{1,0:T(8,128)} fusion(bf16[1024,2048]{0,1:T(8,128)(2,1)} %all-gather.8.cloned.1.call-done, bf16[2048,1024]{1,0:T(8,128)(2,1)} %all-gather.10.cloned.1.call-done), kind=kOutput, calls=%fused_computation.105 | convolution fusion | flops 4294967296 | bytes 12582912 | tf_op jit(solution)/shard_map/dot_general | solution.py:242
  306.1 12.0 %reduce-scatter.2.cloned.1.call-done = f32[1024,512]{1,0:T(8,128)} async-done(((f32[1024,1024]{1,0:T(8,128)}), f32[1024,512]{1,0:T(8,128)}) %reduce-scatter.2.cloned.1.call-update) | async-done | bytes 2097168 | tf_op jit(solution)/shard_map/reduce_scatter | solution.py:243
  318.2 1.7 convert_element_type.45
  319.9 18.3 %all_to_all.5 = bf16[4,256,512]{2,1,0:T(8,128)(2,1)S(1)} all-to-all(bf16[4,256,512]{2,1,0:T(8,128)(2,1)S(1)} %bitcast.149), channel_id=1, replica_groups=mesh['cz'=4,'cb'=4,'head'=2] {'cb'}, dimensions={0} | all-to-all | bytes 2097152 | tf_op jit(solution)/shard_map/all_to_all | solution.py:246
  338.5 1.4 copy.63
  339.8 1.6 reshape.221
  (88 shorter events, 11.3 us)
Async XLA Ops:
  6.5 68.5 %all-gather.12.cloned.1.call-start = ((), (), s32[]{:S(2)}) async-start(), calls=%async_computation.6 | async-start | bytes 1114112 | tf_op jit(solution)/shard_map/all_gather | solution.py:168
  10.6 2.4 collective-permute-start
  12.9 0.6 copy-start.2
  13.0 3.4 copy-start.6
  13.0 3.4 copy-start.7
  13.0 3.4 copy-start.4
  13.2 4.3 %copy-start.1 = (bf16[256,2048]{1,0:T(8,128)(2,1)S(1)}, bf16[256,2048]{1,0:T(8,128)(2,1)}, u32[]{:S(2)}) copy-start(bf16[256,2048]{1,0:T(8,128)(2,1)} %param.13) | copy-start | bytes 3145732
  15.6 147.9 %all-gather.6.cloned.1.call-start = ((), (), s32[]{:S(2)}) async-start(), calls=%async_computation.2 | async-start | bytes 4456448 | tf_op jit(solution)/shard_map/all_gather | solution.py:190
  15.7 0.6 copy-start.5
  17.3 226.5 %all-gather.10.cloned.1.call-start = ((), (), s32[]{:S(2)}) async-start(), calls=%async_computation.4 | async-start | bytes 5242880 | tf_op jit(solution)/shard_map/all_gather | solution.py:241
  20.8 6.0 %collective-permute-start.1 = (bf16[256,4,4,128]{3,0,2,1:T(8,128)(2,1)S(1)}, bf16[256,4,4,128]{3,0,2,1:T(8,128)(2,1)S(1)}, u32[]{:S(2)}, u32[]{:S(2)}) collective-permute-start(bf16[256,4,4,128]{3,0,2,1:T(8,128)(2,1)S(1)} %bitcast.147), channel_id=1, source_target_pairs={{0,1},{1,0},{2,3},{3,2},{4,5},{5,4},{6,7},{7,6},{8,9},{9,8},{10,11... | collective-permute-start | bytes 3145736 | tf_op jit(solution)/shard_map/ppermute | solution.py:135
  20.9 275.2 %all-gather.8.cloned.1.call-start = ((), (), s32[]{:S(2)}) async-start(), calls=%async_computation.3 | async-start | bytes 5242880 | tf_op jit(solution)/shard_map/all_gather | solution.py:240
  21.3 55.2 %collective-permute-start.2 = (bf16[256,2,2,128]{3,0,1,2:T(8,128)(2,1)S(1)}, bf16[256,2,2,128]{3,0,1,2:T(8,128)(2,1)}, u32[]{:S(2)}, u32[]{:S(2)}) collective-permute-start(bf16[256,2,2,128]{3,0,1,2:T(8,128)(2,1)S(1)} %fusion.32), channel_id=1, source_target_pairs={{0,2},{2,4},{4,6},{6,8},{8,10},{10,12},{12,14},{14,16},{16,18},{18... | collective-permute-start | bytes 786440 | tf_op jit(solution)/shard_map/ppermute | solution.py:166
  163.5 10.2 %copy-start.3 = (s32[8]{0:T(128)S(1)}, s32[8]{0:T(128)}, u32[]{:S(2)}) copy-start(s32[8]{0:T(128)} %copy-done.2) | copy-start | bytes 100
  165.8 2.0 copy-start
  173.7 2.7 collective-permute-start.3
  179.0 139.2 %reduce-scatter.2.cloned.1.call-start = ((), (), s32[]{:S(2)}) async-start(), calls=%async_computation.5 | async-start | bytes 6291456 | tf_op jit(solution)/shard_map/reduce_scatter | solution.py:243
Sparse Core Ops, SparseCore 0:
  15.7 59.2 all-gather.11
  77.8 85.6 all-gather.5
  165.0 78.7 all-gather.9
  245.5 50.6 all-gather.7
  306.3 11.8 reduce-scatter.1
